TPU v7x, 128 devices: a whole 4x4x4 slice. The times are simulated.
128 devices in a mesh: group: 8 (over y, core), member: 16 (over z, x).
Axes of the slice: x: 4, y: 4, z: 4, core: 2. Of those that a mesh axis runs over, the one named last changes fastest.
Arguments:
- candidates: bfloat16 [512, 64, 1024], P('member', 'group'), may hold values from -6 to 6
- kv_cache: bfloat16 [64, 2048, 2048], P('group', 'member'), may hold values from -6 to 6
- cache_request: int32 [64], replicated, may hold values from 0 to 63, as said below
- rank_request: int32 [64], replicated, may hold values from 0 to 63, as said below
- hist_blocks: int32 [64], replicated, may hold values from 1 to 16, 544 in all
- w_uq: bfloat16 [1024, 2048], replicated, may hold values from -0.1875 to 0.1875
- w_out: bfloat16 [1024, 1024], replicated, may hold values from -0.1875 to 0.1875
Outputs:
- ranked: bfloat16 [512, 64, 1024], P('member', 'group')
Inputs may be any that keep to these rules, and one draw needn't show every extreme that they name: `cache_request`: A permutation; cache row q lies on group q // 8, events split over member. `rank_request`: A permutation; group g ranks positions g * 8 to (g + 1) * 8 - 1. The requests cached on one group are dealt out to the ranking groups in turn, so every pair of groups carries 8 // 8 or 1 requests and some pair carries exactly 1; the uneven part of the load is the live history lengths.
All inputs are finite; a program needn't handle non-finite values.
Results may differ from a plain program's by a relative error of at most 0.011.
Values may be sent and summed in bfloat16 or wider, within the bound.
No kernel may reach another device: no remote copies, remote signals or barrier semaphores. Data moves between devices by JAX's collectives and lax.ppermute only.
A program may use at most 320 MiB of HBM per device.

v0:
```python
import jax
import jax.numpy as jnp
from jax import lax
from jax.sharding import PartitionSpec as P

HEADS = 8
BLK = 128


def layer_norm(values):
    center = values - jnp.mean(values, axis=-1, keepdims=True)
    spread = jnp.mean(center * center, axis=-1, keepdims=True)
    return center * lax.rsqrt(spread + 1e-05)


def routing(cache_request, rank_request, per_group):
    slot_ids = jnp.arange(cache_request.shape[0], dtype=jnp.int32)
    match = cache_request[:, None] == rank_request[None, :]
    rank_pos = jnp.sum(jnp.where(match, slot_ids[None, :], 0), axis=1)
    target = rank_pos // per_group
    owner_grp = slot_ids // per_group
    earlier = (
        (owner_grp[:, None] == owner_grp[None, :])
        & (target[:, None] == target[None, :])
        & (slot_ids[None, :] < slot_ids[:, None])
    )
    arrival = jnp.sum(earlier.astype(jnp.int32), axis=1)
    slot_of_pos = jnp.sum(jnp.where(match, slot_ids[:, None], 0), axis=0)
    return (target, arrival, slot_of_pos)


def attend(piece, queries, live, scale):
    width = queries.shape[2] * queries.shape[3]
    count = piece.shape[1]
    keys = piece[:, :, :width].reshape(piece.shape[0], count, queries.shape[2], queries.shape[3])
    values = piece[:, :, width:].reshape(piece.shape[0], count, queries.shape[2], queries.shape[3])
    scores = jnp.einsum("crhd,rehd->rhce", queries, keys, preferred_element_type=jnp.float32)
    events = jnp.arange(count).astype(jnp.float32)
    keep = (events[None, :] < live[:, None]).astype(jnp.float32) / live[:, None]
    weights = (jax.nn.silu(scores * scale) * keep[:, None, None, :]).astype(jnp.bfloat16)
    return jnp.einsum("rhce,rehd->crhd", weights, values, preferred_element_type=jnp.float32)


def on_device(candidates, kv_cache, cache_request, rank_request, hist_blocks, w_uq, w_out):
    groups = lax.axis_size("group")
    per_group = kv_cache.shape[0]
    cand_rows = candidates.shape[0]
    width = candidates.shape[2]
    head_dim = width // HEADS
    capacity = (per_group + groups - 1) // groups
    group_now = lax.axis_index("group")
    target, arrival, slot_of_pos = routing(cache_request, rank_request, per_group)
    first_slot = group_now * per_group
    local_target = lax.dynamic_slice_in_dim(target, first_slot, per_group)
    local_arrival = lax.dynamic_slice_in_dim(arrival, first_slot, per_group)
    target_grid = jnp.arange(groups)[:, None, None]
    place_grid = jnp.arange(capacity)[None, :, None]
    hits = (local_target[None, None, :] == target_grid) & (
        local_arrival[None, None, :] == place_grid
    )
    chosen = jnp.sum(jnp.where(hits, jnp.arange(per_group)[None, None, :], 0), axis=2).reshape(-1)
    filled = jnp.any(hits, axis=2).reshape(-1)
    positions = first_slot + jnp.arange(per_group)
    source_slot = slot_of_pos[positions]
    receive_index = source_slot // per_group * capacity + arrival[source_slot]
    live = (hist_blocks[rank_request[positions]] * BLK).astype(jnp.float32)
    inputs = candidates.astype(jnp.float32)
    normed = layer_norm(inputs).astype(jnp.bfloat16).reshape(cand_rows * per_group, width)
    projected = jax.nn.silu(jnp.dot(normed, w_uq, preferred_element_type=jnp.float32))
    gates = projected[:, :width].reshape(cand_rows, per_group, width)
    queries = (
        projected[:, width:].astype(jnp.bfloat16).reshape(cand_rows, per_group, HEADS, head_dim)
    )
    scale = head_dim ** (-0.5)
    outgoing = jnp.where(filled[:, None, None], kv_cache[chosen], jnp.zeros((), jnp.bfloat16))
    incoming = lax.all_to_all(outgoing, "group", split_axis=0, concat_axis=0, tiled=True)
    panels = incoming[receive_index]
    attn = attend(lax.all_gather(panels, "member", axis=1, tiled=True), queries, live, scale)
    attn = attn.reshape(cand_rows, per_group, width)
    gated = (layer_norm(attn) * gates).astype(jnp.bfloat16).reshape(cand_rows * per_group, width)
    result = jnp.dot(gated, w_out, preferred_element_type=jnp.float32) + inputs.reshape(
        cand_rows * per_group, width
    )
    return result.astype(jnp.bfloat16).reshape(cand_rows, per_group, width)


def solution(mesh):
    return jax.shard_map(
        on_device,
        mesh=mesh,
        in_specs=(P("member", "group", None), P("group", "member", None), P(), P(), P(), P(), P()),
        out_specs=P("member", "group", None),
        check_vma=False,
    )
```

profile of v0, /device:TPU:1, one launch (start us, length us, event | category | flops | bytes accessed | tf_op | source)
XLA Modules:
  0.0 615.8 jit_solution(919087667570539489)
XLA Ops:
  6.5 0.0 copy-start
  6.5 1.0 fusion.26
  7.6 0.2 convert_reduce_fusion.1
  7.8 0.1 dynamic_slice.6
  7.8 0.1 dynamic-slice_compare_fusion
  7.9 0.1 select_reduce_fusion
  8.0 0.1 fusion.29
  8.2 5.0 gather_fusion
  13.1 4.5 broadcast_select_fusion
  17.6 6.0 all-to-all-start
  23.6 0.0 all-gather.3.cloned.1.call-start
  23.6 0.6 gather_fusion.1
  24.3 0.6 gather_fusion.2
  25.0 47.4 %all-to-all-done = bf16[8,128,2048]{2,1,0:T(8,128)(2,1)} async-done(((bf16[8,128,2048]{2,1,0:T(8,128)(2,1)}), bf16[8,128,2048]{2,1,0:T(8,128)(2,1)}, u32[]{:S(2)}, u32[]{:S(2)}) %all-to-all-start) | async-done | bytes 4194336 | tf_op jit(solution)/shard_map/all_to_all | solution.py:76
  72.4 5.0 gather_fusion.3
  77.4 0.0 copy-start.1
  77.4 0.0 copy-start.2
  77.4 0.0 copy-start.3
  77.4 0.0 all-gather.3.cloned.1.call-update
  77.4 0.6 copy-done.1
  78.0 0.6 gather_fusion.4
  78.7 0.0 copy-done.2
  78.7 0.6 gather_fusion.5
  79.3 0.0 copy-done.3
  79.3 0.1 convert_reduce_fusion
  79.5 0.3 fusion.8
  79.8 3.7 divide_multiply_fusion
  83.5 0.0 copy-start.4
  83.5 1.3 copy-done.4
  84.8 0.1 fusion.12
  84.9 0.1 convert_divide_fusion
  85.0 361.7 %all-gather.3.cloned.1.call-done = bf16[8,2048,2048]{2,1,0:T(8,128)(2,1)} async-done(((bf16[8,128,2048]{2,1,0:T(8,128)(2,1)}), bf16[8,2048,2048]{2,1,0:T(8,128)(2,1)}) %all-gather.3.cloned.1.call-update) | async-done | bytes 67108880 | tf_op jit(solution)/shard_map/all_gather | solution.py:78
  446.7 43.3 %fusion.37 = (bf16[8,2048,1024]{2,1,0:T(8,128)(2,1)}, bf16[8,2048,1024]{2,1,0:T(8,128)(2,1)}) fusion(bf16[8,2048,2048]{2,1,0:T(8,128)(2,1)} %all-gather.3.cloned.1.call-done), kind=kLoop, calls=%fused_computation.86 | loop fusion | bytes 134217728 | tf_op jit(solution)/shard_map/slice | solution.py:35
  490.0 42.2 %copy.44 = bf16[8,2048,1024]{1,2,0:T(8,128)(2,1)} copy(bf16[8,2048,1024]{2,1,0:T(8,128)(2,1)} %get-tuple-element.7) | data formatting | bytes 67108864 | tf_op jit(solution)/shard_map/slice | solution.py:35
  532.3 42.2 %copy.43 = bf16[8,2048,1024]{1,2,0:T(8,128)(2,1)} copy(bf16[8,2048,1024]{2,1,0:T(8,128)(2,1)} %get-tuple-element.8) | data formatting | bytes 67108864 | tf_op jit(solution)/shard_map/slice | solution.py:36
  574.5 29.0 %fusion.38 = (f32[32,8]{0,1:T(8,128)S(1)}, f32[32,8,8,128]{3,0,2,1:T(8,128)}) fusion(bf16[8,2048,8,128]{1,3,2,0:T(8,128)(2,1)} %bitcast.58, f32[8,2048]{1,0:T(8,128)S(1)} %convert_divide_fusion, bf16[8,2048,8,128]{1,3,2,0:T(8,128)(2,1)} %bitcast.57, bf16[32,8,8,128]{3,1,2,0:T(8,128)(2,1)S(1)} %fusion.12), kind=kOutput, calls=%fused_computation.87 | convolution fusion | flops 2177105664 | bytes 68748288 | tf_op jit(solution)/shard_map/rhce,rehd->crhd/dot_general | solution.py:41
  603.5 0.1 copy.49
  603.6 0.1 copy.50
  603.6 0.1 div.75
  603.7 1.5 multiply_reduce_fusion
  605.2 0.1 copy.51
  605.3 0.1 rsqrt.21
  605.4 0.0 copy-done
  605.4 3.5 fusion.7
  (17 shorter events, 0.1 us)
Async XLA Ops:
  6.5 598.9 %copy-start = (bf16[1024,1024]{1,0:T(8,128)(2,1)S(1)}, bf16[1024,1024]{1,0:T(8,128)(2,1)}, u32[]{:S(2)}) copy-start(bf16[1024,1024]{1,0:T(8,128)(2,1)} %param.13) | copy-start | bytes 6291460
  17.6 54.7 %all-to-all-start = ((bf16[8,128,2048]{2,1,0:T(8,128)(2,1)}), bf16[8,128,2048]{2,1,0:T(8,128)(2,1)}, u32[]{:S(2)}, u32[]{:S(2)}) async-start(bf16[8,128,2048]{2,1,0:T(8,128)(2,1)} %broadcast_select_fusion), calls=%async_computation | async-start | bytes 8388608 | tf_op jit(solution)/shard_map/all_to_all | solution.py:76
  23.6 423.1 %all-gather.3.cloned.1.call-start = ((), (), s32[]{:S(2)}) async-start(), calls=%async_computation.1 | async-start | bytes 71303168 | tf_op jit(solution)/shard_map/all_gather | solution.py:78
  77.4 0.7 copy-start.1
  77.4 1.3 copy-start.2
  77.4 2.0 copy-start.3
  83.5 1.4 copy-start.4
Sparse Core Ops, SparseCore 0:
  77.5 369.1 all-gather.2
where the time goes:
time: 618 us; the launch traced here: 616 us
  waiting for transfers between devices  409 us (66%)
  local copies, waits for them, and re-layouts  143 us (23%)
  matrix products  36.2 us (6%)
  between operations  13.5 us (2%)
  other arithmetic  8.11 us (1%)
    all_gather x1, waiting for transfers between devices, on_device(): lax.all_gather(panels, 'member', axis=1, tiled=True)  362 us
    slice x2, local copies, waits for them, and re-layouts, attend(): piece[:, :, :width]  85.6 us
    all_to_all x1, waiting for transfers between devices, on_device(): lax.all_to_all(outgoing, 'group', split_axis=0, concat_axis=0, tiled=True)  47.4 us
    slice x1, local copies, waits for them, and re-layouts, attend(): piece[:, :, width:]  42.2 us
    dot_general x1, matrix products, attend(): jnp.einsum('rhce,rehd->crhd', weights, values, preferred_element_type=jnp...  29 us
  transfers between devices with their start and end apart: 2, of which 2 were waited for; matrix products, arithmetic and copies ran while one was open for 1% of the time, Pallas kernels for 0%

commit v1 on v0

--- a/solution.py
+++ b/solution.py
@@ -5,6 +5,28 @@
 
 HEADS = 8
 BLK = 128
+
+
+def in_blocks(value, dim, size):
+    before, after = (value.shape[:dim], value.shape[dim + 1 :])
+    return jnp.moveaxis(value.reshape(*before, size, -1, *after), dim, 0)
+
+
+def laid_out(blocks, dim):
+    blocks = jnp.moveaxis(blocks, 0, dim)
+    lengths = blocks.shape
+    return blocks.reshape(*lengths[:dim], lengths[dim] * lengths[dim + 1], *lengths[dim + 2 :])
+
+
+def swapped_with_each(array, axis, split_dim, concat_dim):
+    size, mine = (lax.axis_size(axis), lax.axis_index(axis))
+    blocks = in_blocks(array, split_dim, size)
+    outs = [blocks[mine]]
+    for step in range(1, size):
+        sent = blocks[mine ^ step]
+        outs.append(lax.ppermute(sent, axis, [(i, i ^ step) for i in range(size)]))
+    blocks = jnp.stack(outs)[mine ^ jnp.arange(size)]
+    return laid_out(blocks, concat_dim)
 
 
 def layer_norm(values):
@@ -73,7 +95,7 @@
     )
     scale = head_dim ** (-0.5)
     outgoing = jnp.where(filled[:, None, None], kv_cache[chosen], jnp.zeros((), jnp.bfloat16))
-    incoming = lax.all_to_all(outgoing, "group", split_axis=0, concat_axis=0, tiled=True)
+    incoming = swapped_with_each(outgoing, "group", 0, 0)
     panels = incoming[receive_index]
     attn = attend(lax.all_gather(panels, "member", axis=1, tiled=True), queries, live, scale)
     attn = attn.reshape(cand_rows, per_group, width)

time: 618 us -> 634 us (1.026)
  local copies, waits for them, and re-layouts: 143 us -> 164 us
  waiting for transfers between devices: 409 us -> 395 us
  starting transfers between devices: 5.96 us -> 13.4 us
    all_to_all x1 -> x0, waiting for transfers between devices: 47.4 us -> none  [on_device(): lax.all_to_all(outgoing, 'group', split_axis=0, concat_axis=0, tiled=True)]
    ppermute x0 -> x7, waiting for transfers between devices: none -> 31.5 us  [swapped_with_each(): outs.append(lax.ppermute(sent, axis, [(i, i ^ step) for i in range(size)]))]
    ppermute x0 -> x7, starting transfers between devices: none -> 13.4 us  [swapped_with_each(): outs.append(lax.ppermute(sent, axis, [(i, i ^ step) for i in range(size)]))]
    unnamed x10 -> x17, local copies, waits for them, and re-layouts: 1.98 us -> 14.2 us
  transfers between devices with their start and end apart: 2 -> 8, of which waited for: 2 -> 6; matrix products, arithmetic and copies ran while one was open for 1% -> 3% of each run, Pallas kernels for 0% -> 0%
where the time goes in v1:
time: 634 us; the launch traced here: 631 us
  waiting for transfers between devices  395 us (62%)
  local copies, waits for them, and re-layouts  164 us (26%)
  matrix products  36.4 us (6%)
  between operations  13.6 us (2%)
  starting transfers between devices  13.4 us (2%)
  other arithmetic  8.11 us (1%)
    all_gather x1, waiting for transfers between devices, on_device(): lax.all_gather(panels, 'member', axis=1, tiled=True)  363 us
    slice x2, local copies, waits for them, and re-layouts, attend(): piece[:, :, :width]  85.6 us
    slice x1, local copies, waits for them, and re-layouts, attend(): piece[:, :, width:]  42.2 us
    ppermute x7, waiting for transfers between devices, swapped_with_each(): outs.append(lax.ppermute(sent, axis, [(i, i ^ step) for i in range(size)]))  31.5 us
    dot_general x1, matrix products, attend(): jnp.einsum('rhce,rehd->crhd', weights, values, preferred_element_type=jnp...  29.2 us
    unnamed x17, local copies, waits for them, and re-layouts  14.2 us
    ppermute x7, starting transfers between devices, swapped_with_each(): outs.append(lax.ppermute(sent, axis, [(i, i ^ step) for i in range(size)]))  13.4 us
  transfers between devices with their start and end apart: 8, of which 6 were waited for; matrix products, arithmetic and copies ran while one was open for 3% of the time, Pallas kernels for 0%

profile of v1, /device:TPU:1, one launch (start us, length us, event | category | flops | bytes accessed | tf_op | source)
XLA Modules:
  0.0 630.8 jit_solution(1438096264367936419)
XLA Ops:
  6.5 0.0 copy-start
  6.5 0.0 all-gather.3.cloned.1.call-start
  6.5 1.0 fusion.26
  7.6 0.2 convert_reduce_fusion.1
  7.8 0.1 dynamic_slice.6
  7.8 0.1 dynamic-slice_compare_fusion
  7.9 0.1 select_reduce_fusion
  8.0 0.1 fusion.29
  8.2 5.0 gather_fusion
  13.2 4.5 broadcast_select_fusion
  17.7 0.0 copy-start.1
  17.7 3.6 constant_dynamic-slice_fusion.6
  21.2 1.4 collective-permute-start
  22.6 1.4 collective-permute-start.1
  24.0 0.2 collective-permute-start.2
  24.3 3.0 collective-permute-start.3
  27.3 0.3 collective-permute-start.4
  27.7 0.0 copy-done.1
  27.7 0.6 gather_fusion.5
  28.3 0.6 gather_fusion.2
  29.0 0.6 gather_fusion.3
  29.6 1.9 bitcast_dynamic-update-slice_fusion.7
  31.5 0.0 collective-permute-done
  31.5 2.9 collective-permute-start.5
  34.5 1.9 bitcast_dynamic-update-slice_fusion.6
  36.4 0.1 collective-permute-done.1
  36.4 4.1 collective-permute-start.6
  40.5 1.9 bitcast_dynamic-update-slice_fusion.5
  42.4 6.1 collective-permute-done.2
  48.5 1.9 bitcast_dynamic-update-slice_fusion.4
  50.4 11.1 %collective-permute-done.3 = bf16[1,128,2048]{2,1,0:T(8,128)(2,1)} collective-permute-done((bf16[1,128,2048]{2,1,0:T(8,128)(2,1)}, bf16[1,128,2048]{2,1,0:T(8,128)(2,1)}, u32[]{:S(2)}, u32[]{:S(2)}) %collective-permute-start.3) | collective-permute-done | bytes 524320 | tf_op jit(solution)/shard_map/ppermute | solution.py:27
  61.5 1.9 bitcast_dynamic-update-slice_fusion.3
  63.4 9.6 %collective-permute-done.4 = bf16[1,128,2048]{2,1,0:T(8,128)(2,1)} collective-permute-done((bf16[1,128,2048]{2,1,0:T(8,128)(2,1)}, bf16[1,128,2048]{2,1,0:T(8,128)(2,1)}, u32[]{:S(2)}, u32[]{:S(2)}) %collective-permute-start.4) | collective-permute-done | bytes 524320 | tf_op jit(solution)/shard_map/ppermute | solution.py:27
  73.0 1.9 bitcast_dynamic-update-slice_fusion.2
  74.9 0.0 collective-permute-done.5
  74.9 0.8 bitcast_dynamic-update-slice_fusion.1
  75.7 4.7 collective-permute-done.6
  80.4 0.8 bitcast_dynamic-update-slice_fusion
  81.2 5.0 gather_fusion.1
  86.2 5.0 gather_fusion.4
  91.2 0.0 all-gather.3.cloned.1.call-update
  91.2 0.6 copy-done.2
  91.8 0.6 gather_fusion.6
  92.5 0.0 copy-done.3
  92.5 0.1 convert_reduce_fusion
  92.6 0.3 fusion.8
  92.9 3.7 divide_multiply_fusion
  96.6 0.0 copy-start.4
  96.6 1.3 copy-done.4
  97.9 0.1 fusion.12
  98.0 0.1 convert_divide_fusion
  98.1 363.4 %all-gather.3.cloned.1.call-done = bf16[8,2048,2048]{2,1,0:T(8,128)(2,1)} async-done(((bf16[8,128,2048]{2,1,0:T(8,128)(2,1)}), bf16[8,2048,2048]{2,1,0:T(8,128)(2,1)}) %all-gather.3.cloned.1.call-update) | async-done | bytes 67108880 | tf_op jit(solution)/shard_map/all_gather | solution.py:100
  461.5 43.3 %fusion.38 = (bf16[8,2048,1024]{2,1,0:T(8,128)(2,1)}, bf16[8,2048,1024]{2,1,0:T(8,128)(2,1)}) fusion(bf16[8,2048,2048]{2,1,0:T(8,128)(2,1)} %all-gather.3.cloned.1.call-done), kind=kLoop, calls=%fused_computation.105 | loop fusion | bytes 134217728 | tf_op jit(solution)/shard_map/slice | solution.py:57
  504.8 42.2 %copy.43 = bf16[8,2048,1024]{1,2,0:T(8,128)(2,1)} copy(bf16[8,2048,1024]{2,1,0:T(8,128)(2,1)} %get-tuple-element.8) | data formatting | bytes 67108864 | tf_op jit(solution)/shard_map/slice | solution.py:58
  547.1 42.2 %copy.44 = bf16[8,2048,1024]{1,2,0:T(8,128)(2,1)} copy(bf16[8,2048,1024]{2,1,0:T(8,128)(2,1)} %get-tuple-element.7) | data formatting | bytes 67108864 | tf_op jit(solution)/shard_map/slice | solution.py:57
  589.3 29.2 %fusion.39 = (f32[32,8]{0,1:T(8,128)S(1)}, f32[32,8,8,128]{3,0,2,1:T(8,128)}) fusion(bf16[8,2048,8,128]{1,3,2,0:T(8,128)(2,1)} %bitcast.76, f32[8,2048]{1,0:T(8,128)S(1)} %convert_divide_fusion, bf16[8,2048,8,128]{1,3,2,0:T(8,128)(2,1)} %bitcast.77, bf16[32,8,8,128]{3,1,2,0:T(8,128)(2,1)S(1)} %fusion.12), kind=kOutput, calls=%fused_computation.106 | convolution fusion | flops 2177105664 | bytes 68748288 | tf_op jit(solution)/shard_map/rhce,rehd->crhd/dot_general | solution.py:63
  618.5 0.1 copy.49
  618.6 0.1 copy.50
  618.7 0.1 div.75
  618.8 1.5 multiply_reduce_fusion
  620.2 0.1 copy.51
  620.3 0.1 rsqrt.21
  620.4 0.0 copy-done
  620.4 3.5 fusion.7
  (20 shorter events, 0.1 us)
Async XLA Ops:
  6.5 613.9 %copy-start = (bf16[1024,1024]{1,0:T(8,128)(2,1)S(1)}, bf16[1024,1024]{1,0:T(8,128)(2,1)}, u32[]{:S(2)}) copy-start(bf16[1024,1024]{1,0:T(8,128)(2,1)} %param.13) | copy-start | bytes 6291460
  6.5 455.0 %all-gather.3.cloned.1.call-start = ((), (), s32[]{:S(2)}) async-start(), calls=%async_computation | async-start | bytes 71303168 | tf_op jit(solution)/shard_map/all_gather | solution.py:100
  17.7 10.0 %copy-start.1 = (s32[64]{0:T(128)S(1)}, s32[64]{0:T(128)}, u32[]{:S(2)}) copy-start(s32[64]{0:T(128)} %param.10) | copy-start | bytes 772
  21.2 10.3 %collective-permute-start = (bf16[1,128,2048]{2,1,0:T(8,128)(2,1)}, bf16[1,128,2048]{2,1,0:T(8,128)(2,1)}, u32[]{:S(2)}, u32[]{:S(2)}) collective-permute-start(bf16[1,128,2048]{2,1,0:T(8,128)(2,1)} %get-tuple-element.15), channel_id=1, source_target_pairs={{0,16},{16,0},{32,48},{48,32},{64,80},{80,64},{96,112},{112,96},{1... | collective-permute-start | bytes 1572872 | tf_op jit(solution)/shard_map/ppermute | solution.py:27
  22.6 13.8 %collective-permute-start.1 = (bf16[1,128,2048]{2,1,0:T(8,128)(2,1)}, bf16[1,128,2048]{2,1,0:T(8,128)(2,1)}, u32[]{:S(2)}, u32[]{:S(2)}) collective-permute-start(bf16[1,128,2048]{2,1,0:T(8,128)(2,1)} %get-tuple-element.14), channel_id=1, source_target_pairs={{0,32},{16,48},{32,0},{48,16},{64,96},{80,112},{96,64},{112,80},{1... | collective-permute-start | bytes 1572872 | tf_op jit(solution)/shard_map/ppermute | solution.py:27
  24.0 24.4 %collective-permute-start.2 = (bf16[1,128,2048]{2,1,0:T(8,128)(2,1)}, bf16[1,128,2048]{2,1,0:T(8,128)(2,1)}, u32[]{:S(2)}, u32[]{:S(2)}) collective-permute-start(bf16[1,128,2048]{2,1,0:T(8,128)(2,1)} %get-tuple-element.13), channel_id=1, source_target_pairs={{0,48},{16,32},{32,16},{48,0},{64,112},{80,96},{96,80},{112,64},{1... | collective-permute-start | bytes 1572872 | tf_op jit(solution)/shard_map/ppermute | solution.py:27
  24.3 37.2 %collective-permute-start.3 = (bf16[1,128,2048]{2,1,0:T(8,128)(2,1)}, bf16[1,128,2048]{2,1,0:T(8,128)(2,1)}, u32[]{:S(2)}, u32[]{:S(2)}) collective-permute-start(bf16[1,128,2048]{2,1,0:T(8,128)(2,1)} %get-tuple-element.12), channel_id=1, source_target_pairs={{0,64},{16,80},{32,96},{48,112},{64,0},{80,16},{96,32},{112,48},{1... | collective-permute-start | bytes 1572872 | tf_op jit(solution)/shard_map/ppermute | solution.py:27
  27.3 45.7 %collective-permute-start.4 = (bf16[1,128,2048]{2,1,0:T(8,128)(2,1)}, bf16[1,128,2048]{2,1,0:T(8,128)(2,1)}, u32[]{:S(2)}, u32[]{:S(2)}) collective-permute-start(bf16[1,128,2048]{2,1,0:T(8,128)(2,1)} %get-tuple-element.11), channel_id=1, source_target_pairs={{0,80},{16,64},{32,112},{48,96},{64,16},{80,0},{96,48},{112,32},{1... | collective-permute-start | bytes 1572872 | tf_op jit(solution)/shard_map/ppermute | solution.py:27
  31.5 43.3 %collective-permute-start.5 = (bf16[1,128,2048]{2,1,0:T(8,128)(2,1)S(1)}, bf16[1,128,2048]{2,1,0:T(8,128)(2,1)S(1)}, u32[]{:S(2)}, u32[]{:S(2)}) collective-permute-start(bf16[1,128,2048]{2,1,0:T(8,128)(2,1)S(1)} %get-tuple-element.10), channel_id=1, source_target_pairs={{0,96},{16,112},{32,64},{48,80},{64,32},{80,48},{96,0},{112,16},{1... | collective-permute-start | bytes 1572872 | tf_op jit(solution)/shard_map/ppermute | solution.py:27
  36.4 43.9 %collective-permute-start.6 = (bf16[1,128,2048]{2,1,0:T(8,128)(2,1)S(1)}, bf16[1,128,2048]{2,1,0:T(8,128)(2,1)S(1)}, u32[]{:S(2)}, u32[]{:S(2)}) collective-permute-start(bf16[1,128,2048]{2,1,0:T(8,128)(2,1)S(1)} %get-tuple-element.9), channel_id=1, source_target_pairs={{0,112},{16,96},{32,80},{48,64},{64,48},{80,32},{96,16},{112,0},{1... | collective-permute-start | bytes 1572872 | tf_op jit(solution)/shard_map/ppermute | solution.py:27
  91.2 0.7 copy-start.2
  91.2 1.3 copy-start.3
  96.6 1.4 copy-start.4
Sparse Core Ops, SparseCore 0:
  91.3 370.1 all-gather.2
